TPU v7x, 32 devices: a whole 2x2x4 slice. The times are simulated.
32 devices in a mesh: groups: 2 (over y), section: 4 (over x, core), filt: 4 (over z).
Axes of the slice: x: 2, y: 2, z: 4, core: 2. Of those that a mesh axis runs over, the one named last changes fastest.
Arguments:
- volumes: bfloat16 [16, 256, 4, 2, 128], P('groups', 'filt'), parts along dimension 0, may hold values from -6 to 6
- weights: bfloat16 [4, 256, 27, 256], P('section', 'filt'), may hold values from -0.125 to 0.125
- biases: float32 [4, 256], P('section', 'filt'), may hold values from -3 to 3
- cotangent: bfloat16 [16, 256, 4, 2, 128], P('groups', 'filt'), parts along dimension 0, may hold values from -6 to 6
Outputs:
- grad_weights: float32 [8, 256, 27, 256], P(('groups', 'section'), 'filt'), parts along dimension 0
- grad_biases: float32 [8, 256], P(('groups', 'section'), 'filt'), parts along dimension 0
- grad_inputs: bfloat16 [8, 8, 256, 4, 2, 128], P(('groups', 'section'), None, 'filt'), parts along dimension 0
There are 2 independent parts, one for each index of `groups`. A program takes and returns all parts, laid end to end along the dimension named above; an argument that names none is the same for every part. Nothing has to cross between parts.
All inputs are finite; a program needn't handle non-finite values.
Results may differ from a plain program's by a relative error of at most 0.019.
Values may be sent and summed in bfloat16 or wider, within the bound.
No kernel may reach another device: no remote copies, remote signals or barrier semaphores. Data moves between devices by JAX's collectives and lax.ppermute only.
A program may use at most 64 MiB of HBM per device.

v0:
```python
import math
import jax
import jax.numpy as jnp
import numpy as np
from jax import lax
from jax.sharding import PartitionSpec as P

tap_offsets = [
    (first, second, third) for first in (-1, 0, 1) for second in (-1, 0, 1) for third in (-1, 0, 1)
]


def passed_along(value, axis, steps):
    count = lax.axis_size(axis)
    first, last = (max(0, -steps), min(count, count - steps))
    return lax.ppermute(value, axis, [(source, source + steps) for source in range(first, last)])


def for_sending(x):
    return jax.tree.map(lambda a: a.astype(jnp.bfloat16) if a.dtype == jnp.float32 else a, x)


def lane_shift(values, step):
    if step == 0:
        return values
    width = values.shape[-1]
    source = jnp.arange(width)[:, None]
    target = jnp.arange(width)[None, :]
    if values.dtype == jnp.float32:
        matrix = (source == target + step).astype(jnp.float32)
        return jnp.einsum(
            "...z,zw->...w",
            values,
            matrix,
            precision=lax.Precision.HIGHEST,
            preferred_element_type=jnp.float32,
        )
    matrix = (source == target + step).astype(values.dtype)
    return jnp.einsum("...z,zw->...w", values, matrix, preferred_element_type=jnp.float32).astype(
        values.dtype
    )


def row_shift(values, step_x, step_y, extent_x, extent_y):
    if step_x == 0 and step_y == 0:
        return values
    row_total = extent_x * extent_y
    delta = step_x * extent_y + step_y
    keep_mask = np.zeros((row_total, 1), dtype=bool)
    for row_pos in range(row_total):
        pos_x = row_pos // extent_y + step_x
        pos_y = row_pos % extent_y + step_y
        keep_mask[row_pos, 0] = 0 <= pos_x < extent_x and 0 <= pos_y < extent_y
    margin = extent_y + 1
    padded = jnp.pad(values, [(0, 0)] * (values.ndim - 2) + [(margin, margin), (0, 0)])
    sliced = lax.slice_in_dim(
        padded, margin + delta, margin + delta + row_total, axis=values.ndim - 2
    )
    return jnp.where(jnp.asarray(keep_mask), sliced, jnp.zeros((), values.dtype))


def sum_taps(product, direction, extent_x, extent_y):
    summed = jnp.zeros(product.shape[:1] + product.shape[2:], jnp.float32)
    for lane_step in (-1, 0, 1):
        partial_sum = jnp.zeros(product.shape[:1] + product.shape[2:], jnp.float32)
        for tap_index, offset in enumerate(tap_offsets):
            if offset[2] == lane_step:
                partial_sum = partial_sum + row_shift(
                    product[:, tap_index],
                    direction * offset[0],
                    direction * offset[1],
                    extent_x,
                    extent_y,
                )
        summed = summed + lane_shift(partial_sum, direction * lane_step)
    return summed


def stack_taps(values, direction, extent_x, extent_y):
    shifted_lanes = {}
    for lane_step in (-1, 0, 1):
        shifted_lanes[lane_step] = lane_shift(values, direction * lane_step)
    return jnp.stack(
        [
            row_shift(
                shifted_lanes[offset[2]],
                direction * offset[0],
                direction * offset[1],
                extent_x,
                extent_y,
            )
            for offset in tap_offsets
        ],
        axis=1,
    )


def silu_slope(pre_act):
    sigmoid = jax.nn.sigmoid(pre_act)
    return sigmoid * (1.0 + pre_act * (1.0 - sigmoid))


def store_slot(buffer, entry, position, in_range):
    previous = lax.dynamic_index_in_dim(buffer, position, 0, keepdims=False)
    return lax.dynamic_update_index_in_dim(
        buffer, jnp.where(in_range, entry, previous), position, 0
    )


def local(volumes, weights, biases, cotangent):
    section_count = lax.axis_size("section")
    section_pos = lax.axis_index("section")
    micro_count = volumes.shape[0]
    tick_count = micro_count + section_count - 1
    weight = weights[0]
    own_count, tap_count, channels = weight.shape
    weight_rows = weight.reshape(own_count * tap_count, channels)
    layer_bias = biases[0]
    extent_x, extent_y, lane_count = volumes.shape[2:]
    row_total = extent_x * extent_y
    cell_count = row_total * lane_count
    flat_volumes = volumes.reshape(micro_count, own_count, row_total, lane_count)
    flat_cotangent = cotangent.reshape(micro_count, own_count, row_total, lane_count)
    stored = jnp.zeros((micro_count, own_count, row_total, lane_count), jnp.bfloat16)
    saved_pre = jnp.zeros((micro_count, own_count, row_total, lane_count), jnp.float32)
    empty_slab = jnp.zeros((own_count, row_total, lane_count), jnp.bfloat16)

    def forward_tick(tick_now, carried):
        incoming, saved_pre, stored = carried
        sample = tick_now - section_pos
        in_range = (sample >= 0) & (sample < micro_count)
        position = jnp.clip(sample, 0, micro_count - 1)
        first_input = lax.dynamic_index_in_dim(flat_volumes, position, 0, keepdims=False)
        own_input = jnp.where(section_pos == 0, first_input, incoming)
        panel_part = jax.tree.map(
            lambda a: lax.all_gather(a, "filt", axis=0, tiled=True), own_input
        )
        columns = lax.slice_in_dim(weight_rows, 0, panel_part.shape[0], axis=1)
        product = jnp.zeros(
            (own_count * tap_count, row_total, lane_count), jnp.float32
        ) + jnp.einsum("ki,irz->krz", columns, panel_part, preferred_element_type=jnp.float32)
        stored = store_slot(stored, own_input, position, in_range)
        pre_act = (
            sum_taps(
                product.reshape(own_count, tap_count, row_total, lane_count), 1, extent_x, extent_y
            )
            + layer_bias[:, None, None]
        )
        saved_pre = store_slot(saved_pre, pre_act, position, in_range)
        outgoing = jax.nn.silu(pre_act).astype(jnp.bfloat16)
        incoming = passed_along(outgoing, "section", 1)
        return (incoming, saved_pre, stored)

    unused_slab, saved_pre, stored = lax.fori_loop(
        0, tick_count, forward_tick, (empty_slab, saved_pre, stored)
    )

    def backward_tick(tick_now, carried):
        incoming, grad_rows, grad_bias, grad_in = carried
        sample = tick_now - (section_count - 1 - section_pos)
        in_range = (sample >= 0) & (sample < micro_count)
        position = jnp.clip(sample, 0, micro_count - 1)
        last_grad = lax.dynamic_index_in_dim(flat_cotangent, position, 0, keepdims=False)
        upstream = jnp.where(section_pos == section_count - 1, last_grad, incoming)
        pre_act = lax.dynamic_index_in_dim(saved_pre, position, 0, keepdims=False)
        slope_grad = (upstream.astype(jnp.float32) * silu_slope(pre_act)).astype(jnp.bfloat16)
        stacked = stack_taps(slope_grad, -1, extent_x, extent_y).reshape(
            own_count * tap_count, row_total, lane_count
        )
        own_input = lax.dynamic_index_in_dim(stored, position, 0, keepdims=False)
        weight_term = jnp.einsum(
            "krz,irz->ki",
            stacked,
            lax.all_gather(for_sending(own_input), "filt", axis=0, tiled=True),
            preferred_element_type=jnp.float32,
        )
        grad_rows = grad_rows + jnp.where(in_range, weight_term, 0.0)
        grad_bias = grad_bias + jnp.where(
            in_range, jnp.sum(slope_grad.astype(jnp.float32), axis=(1, 2)), 0.0
        )
        columns = lax.slice_in_dim(weight_rows, 0, own_count * lax.axis_size("filt"), axis=1)
        input_grad = lax.psum_scatter(
            jnp.einsum("ki,krz->irz", columns, stacked, preferred_element_type=jnp.float32).astype(
                jnp.bfloat16
            ),
            "filt",
            scatter_dimension=0,
            tiled=True,
        ).astype(jnp.float32)
        input_grad = input_grad.astype(jnp.bfloat16)
        grad_in = store_slot(grad_in, input_grad, position, in_range)
        incoming = passed_along(input_grad, "section", -1)
        return (incoming, grad_rows, grad_bias, grad_in)

    start_state = (
        empty_slab,
        jnp.zeros((own_count * tap_count, channels), jnp.float32),
        jnp.zeros((own_count,), jnp.float32),
        jnp.zeros((micro_count, own_count, row_total, lane_count), jnp.bfloat16),
    )
    unused_grad, grad_rows, grad_bias, grad_in = lax.fori_loop(
        0, tick_count, backward_tick, start_state
    )
    norm_scale = 1.0 / math.sqrt(micro_count * cell_count)
    grad_out = grad_in.reshape(1, micro_count, own_count, extent_x, extent_y, lane_count)
    return (
        (grad_rows * norm_scale).reshape(1, own_count, tap_count, channels),
        (grad_bias * norm_scale)[None],
        grad_out,
    )


def solution(mesh):
    in_specs = (
        P("groups", "filt", None, None, None),
        P("section", "filt", None, None),
        P("section", "filt"),
        P("groups", "filt", None, None, None),
    )
    out_specs = (
        P(("groups", "section"), "filt", None, None),
        P(("groups", "section"), "filt"),
        P(("groups", "section"), None, "filt", None, None, None),
    )
    return jax.shard_map(local, mesh=mesh, in_specs=in_specs, out_specs=out_specs, check_vma=False)
```

profile of v0, /device:TPU:1, one launch (start us, length us, event | category | flops | bytes accessed | tf_op | source)
XLA Modules:
  0.0 1059.6 jit_solution(5570250423504639003)
XLA Ops:
  13.4 434.8 %while.45 = (s32[]{:T(128)}, bf16[64,8,128]{2,0,1:T(8,128)(2,1)S(1)}, f32[8,64,8,128]{3,1,2,0:T(8,128)}, bf16[8,64,8,128]{3,1,2,0:T(8,128)(2,1)}, pred[]{:T(512)...) while((s32[]{:T(128)}, ...), condition=%wide.region_1.2_spmd.clone.clone, body=%wide.region_0.1_spmd.sunk.clone.clone.sunk | while | flops 1111195904 | bytes 60796016 | solution.py:154
  15.1 15.3 %all_gather.26 = bf16[256,8,128]{2,0,1:T(8,128)(2,1)S(1)} all-gather(bf16[64,8,128]{2,0,1:T(8,128)(2,1)S(1)} %get-tuple-element.2151), channel_id=1, replica_groups=mesh['groups'=2,'section'=4,'filt'=4] {'filt'}, dimensions={0}, use_global_device_ids=true | all-gather | bytes 655360 | tf_op jit(solution)/shard_map/while/body/eval_jaxpr/all_gather | solution.py:136
  55.4 14.9 %all_gather.26 = bf16[256,8,128]{2,0,1:T(8,128)(2,1)S(1)} all-gather(bf16[64,8,128]{2,0,1:T(8,128)(2,1)S(1)} %get-tuple-element.2151), channel_id=1, replica_groups=mesh['groups'=2,'section'=4,'filt'=4] {'filt'}, dimensions={0}, use_global_device_ids=true | all-gather | bytes 655360 | tf_op jit(solution)/shard_map/while/body/eval_jaxpr/all_gather | solution.py:136
  95.9 13.3 %all_gather.26 = bf16[256,8,128]{2,0,1:T(8,128)(2,1)S(1)} all-gather(bf16[64,8,128]{2,0,1:T(8,128)(2,1)S(1)} %get-tuple-element.2151), channel_id=1, replica_groups=mesh['groups'=2,'section'=4,'filt'=4] {'filt'}, dimensions={0}, use_global_device_ids=true | all-gather | bytes 655360 | tf_op jit(solution)/shard_map/while/body/eval_jaxpr/all_gather | solution.py:136
  136.1 13.0 %all_gather.26 = bf16[256,8,128]{2,0,1:T(8,128)(2,1)S(1)} all-gather(bf16[64,8,128]{2,0,1:T(8,128)(2,1)S(1)} %get-tuple-element.2151), channel_id=1, replica_groups=mesh['groups'=2,'section'=4,'filt'=4] {'filt'}, dimensions={0}, use_global_device_ids=true | all-gather | bytes 655360 | tf_op jit(solution)/shard_map/while/body/eval_jaxpr/all_gather | solution.py:136
  175.2 12.9 %all_gather.26 = bf16[256,8,128]{2,0,1:T(8,128)(2,1)S(1)} all-gather(bf16[64,8,128]{2,0,1:T(8,128)(2,1)S(1)} %get-tuple-element.2151), channel_id=1, replica_groups=mesh['groups'=2,'section'=4,'filt'=4] {'filt'}, dimensions={0}, use_global_device_ids=true | all-gather | bytes 655360 | tf_op jit(solution)/shard_map/while/body/eval_jaxpr/all_gather | solution.py:136
  214.5 12.4 %all_gather.26 = bf16[256,8,128]{2,0,1:T(8,128)(2,1)S(1)} all-gather(bf16[64,8,128]{2,0,1:T(8,128)(2,1)S(1)} %get-tuple-element.2151), channel_id=1, replica_groups=mesh['groups'=2,'section'=4,'filt'=4] {'filt'}, dimensions={0}, use_global_device_ids=true | all-gather | bytes 655360 | tf_op jit(solution)/shard_map/while/body/eval_jaxpr/all_gather | solution.py:136
  253.6 13.0 %all_gather.26 = bf16[256,8,128]{2,0,1:T(8,128)(2,1)S(1)} all-gather(bf16[64,8,128]{2,0,1:T(8,128)(2,1)S(1)} %get-tuple-element.2151), channel_id=1, replica_groups=mesh['groups'=2,'section'=4,'filt'=4] {'filt'}, dimensions={0}, use_global_device_ids=true | all-gather | bytes 655360 | tf_op jit(solution)/shard_map/while/body/eval_jaxpr/all_gather | solution.py:136
  293.0 12.6 %all_gather.26 = bf16[256,8,128]{2,0,1:T(8,128)(2,1)S(1)} all-gather(bf16[64,8,128]{2,0,1:T(8,128)(2,1)S(1)} %get-tuple-element.2151), channel_id=1, replica_groups=mesh['groups'=2,'section'=4,'filt'=4] {'filt'}, dimensions={0}, use_global_device_ids=true | all-gather | bytes 655360 | tf_op jit(solution)/shard_map/while/body/eval_jaxpr/all_gather | solution.py:136
  332.1 12.6 %all_gather.26 = bf16[256,8,128]{2,0,1:T(8,128)(2,1)S(1)} all-gather(bf16[64,8,128]{2,0,1:T(8,128)(2,1)S(1)} %get-tuple-element.2151), channel_id=1, replica_groups=mesh['groups'=2,'section'=4,'filt'=4] {'filt'}, dimensions={0}, use_global_device_ids=true | all-gather | bytes 655360 | tf_op jit(solution)/shard_map/while/body/eval_jaxpr/all_gather | solution.py:136
  371.4 12.2 %all_gather.26 = bf16[256,8,128]{2,0,1:T(8,128)(2,1)S(1)} all-gather(bf16[64,8,128]{2,0,1:T(8,128)(2,1)S(1)} %get-tuple-element.2151), channel_id=1, replica_groups=mesh['groups'=2,'section'=4,'filt'=4] {'filt'}, dimensions={0}, use_global_device_ids=true | all-gather | bytes 655360 | tf_op jit(solution)/shard_map/while/body/eval_jaxpr/all_gather | solution.py:136
  410.5 12.2 %all_gather.26 = bf16[256,8,128]{2,0,1:T(8,128)(2,1)S(1)} all-gather(bf16[64,8,128]{2,0,1:T(8,128)(2,1)S(1)} %get-tuple-element.2151), channel_id=1, replica_groups=mesh['groups'=2,'section'=4,'filt'=4] {'filt'}, dimensions={0}, use_global_device_ids=true | all-gather | bytes 655360 | tf_op jit(solution)/shard_map/while/body/eval_jaxpr/all_gather | solution.py:136
  449.3 596.6 %while.46 = (s32[]{:T(128)}, bf16[64,8,128]{2,1,0:T(8,128)(2,1)S(1)}, f32[1728,256]{1,0:T(8,128)}, f32[64]{0:T(128)}, bf16[8,64,8,128]{3,2,1,0:T(8,128)(2,1)}, /...) while((s32[]{:T(128)}, ...), condition=%wide.region_5.6_spmd.clone.clone.clone, body=%wide.region_2.5_spmd.sunk.clone.clone.clone.sunk | while | flops 1849737728 | bytes 33530844 | solution.py:201
  472.5 18.2 %all-gather.4 = bf16[1,256,8,128]{3,1,2,0:T(8,128)(2,1)S(1)} all-gather(bf16[1,64,8,128]{3,1,2,0:T(8,128)(2,1)} %constant_dynamic-slice_fusion.13), channel_id=2, replica_groups=mesh['groups'=2,'section'=4,'filt'=4] {'filt'}, dimensions={1}, use_global_device_ids=true | all-gather | bytes 655360 | tf_op jit(solution)/shard_map/while/body/eval_jaxpr/all_gather | solution.py:174
  525.9 20.0 %all-gather.4 = bf16[1,256,8,128]{3,1,2,0:T(8,128)(2,1)S(1)} all-gather(bf16[1,64,8,128]{3,1,2,0:T(8,128)(2,1)} %constant_dynamic-slice_fusion.13), channel_id=2, replica_groups=mesh['groups'=2,'section'=4,'filt'=4] {'filt'}, dimensions={1}, use_global_device_ids=true | all-gather | bytes 655360 | tf_op jit(solution)/shard_map/while/body/eval_jaxpr/all_gather | solution.py:174
  580.5 20.0 %all-gather.4 = bf16[1,256,8,128]{3,1,2,0:T(8,128)(2,1)S(1)} all-gather(bf16[1,64,8,128]{3,1,2,0:T(8,128)(2,1)} %constant_dynamic-slice_fusion.13), channel_id=2, replica_groups=mesh['groups'=2,'section'=4,'filt'=4] {'filt'}, dimensions={1}, use_global_device_ids=true | all-gather | bytes 655360 | tf_op jit(solution)/shard_map/while/body/eval_jaxpr/all_gather | solution.py:174
  635.1 19.3 %all-gather.4 = bf16[1,256,8,128]{3,1,2,0:T(8,128)(2,1)S(1)} all-gather(bf16[1,64,8,128]{3,1,2,0:T(8,128)(2,1)} %constant_dynamic-slice_fusion.13), channel_id=2, replica_groups=mesh['groups'=2,'section'=4,'filt'=4] {'filt'}, dimensions={1}, use_global_device_ids=true | all-gather | bytes 655360 | tf_op jit(solution)/shard_map/while/body/eval_jaxpr/all_gather | solution.py:174
  689.0 20.1 %all-gather.4 = bf16[1,256,8,128]{3,1,2,0:T(8,128)(2,1)S(1)} all-gather(bf16[1,64,8,128]{3,1,2,0:T(8,128)(2,1)} %constant_dynamic-slice_fusion.13), channel_id=2, replica_groups=mesh['groups'=2,'section'=4,'filt'=4] {'filt'}, dimensions={1}, use_global_device_ids=true | all-gather | bytes 655360 | tf_op jit(solution)/shard_map/while/body/eval_jaxpr/all_gather | solution.py:174
  743.7 19.2 %all-gather.4 = bf16[1,256,8,128]{3,1,2,0:T(8,128)(2,1)S(1)} all-gather(bf16[1,64,8,128]{3,1,2,0:T(8,128)(2,1)} %constant_dynamic-slice_fusion.13), channel_id=2, replica_groups=mesh['groups'=2,'section'=4,'filt'=4] {'filt'}, dimensions={1}, use_global_device_ids=true | all-gather | bytes 655360 | tf_op jit(solution)/shard_map/while/body/eval_jaxpr/all_gather | solution.py:174
  797.5 20.0 %all-gather.4 = bf16[1,256,8,128]{3,1,2,0:T(8,128)(2,1)S(1)} all-gather(bf16[1,64,8,128]{3,1,2,0:T(8,128)(2,1)} %constant_dynamic-slice_fusion.13), channel_id=2, replica_groups=mesh['groups'=2,'section'=4,'filt'=4] {'filt'}, dimensions={1}, use_global_device_ids=true | all-gather | bytes 655360 | tf_op jit(solution)/shard_map/while/body/eval_jaxpr/all_gather | solution.py:174
  852.1 19.3 %all-gather.4 = bf16[1,256,8,128]{3,1,2,0:T(8,128)(2,1)S(1)} all-gather(bf16[1,64,8,128]{3,1,2,0:T(8,128)(2,1)} %constant_dynamic-slice_fusion.13), channel_id=2, replica_groups=mesh['groups'=2,'section'=4,'filt'=4] {'filt'}, dimensions={1}, use_global_device_ids=true | all-gather | bytes 655360 | tf_op jit(solution)/shard_map/while/body/eval_jaxpr/all_gather | solution.py:174
  906.0 20.0 %all-gather.4 = bf16[1,256,8,128]{3,1,2,0:T(8,128)(2,1)S(1)} all-gather(bf16[1,64,8,128]{3,1,2,0:T(8,128)(2,1)} %constant_dynamic-slice_fusion.13), channel_id=2, replica_groups=mesh['groups'=2,'section'=4,'filt'=4] {'filt'}, dimensions={1}, use_global_device_ids=true | all-gather | bytes 655360 | tf_op jit(solution)/shard_map/while/body/eval_jaxpr/all_gather | solution.py:174
  960.7 19.2 %all-gather.4 = bf16[1,256,8,128]{3,1,2,0:T(8,128)(2,1)S(1)} all-gather(bf16[1,64,8,128]{3,1,2,0:T(8,128)(2,1)} %constant_dynamic-slice_fusion.13), channel_id=2, replica_groups=mesh['groups'=2,'section'=4,'filt'=4] {'filt'}, dimensions={1}, use_global_device_ids=true | all-gather | bytes 655360 | tf_op jit(solution)/shard_map/while/body/eval_jaxpr/all_gather | solution.py:174
  1014.4 20.0 %all-gather.4 = bf16[1,256,8,128]{3,1,2,0:T(8,128)(2,1)S(1)} all-gather(bf16[1,64,8,128]{3,1,2,0:T(8,128)(2,1)} %constant_dynamic-slice_fusion.13), channel_id=2, replica_groups=mesh['groups'=2,'section'=4,'filt'=4] {'filt'}, dimensions={1}, use_global_device_ids=true | all-gather | bytes 655360 | tf_op jit(solution)/shard_map/while/body/eval_jaxpr/all_gather | solution.py:174
  (820 shorter events, 683.0 us)
Async XLA Ops:
  46.7 7.0 collective-permute-start
  86.6 7.7 collective-permute-start
  125.6 8.9 collective-permute-start
  165.4 8.2 collective-permute-start
  204.3 8.5 collective-permute-start
  243.2 8.8 collective-permute-start
  282.9 8.4 collective-permute-start
  321.8 8.6 collective-permute-start
  360.9 8.8 collective-permute-start
  399.9 9.0 collective-permute-start
  439.0 9.2 collective-permute-start
  449.4 44.2 %reduce-scatter.2.cloned.1.call-start = ((), (), s32[]{:S(2)}) async-start(), calls=%async_computation.1 | async-start | bytes 655360 | tf_op jit(solution)/shard_map/while/body/eval_jaxpr/reduce_scatter | solution.py:182
  493.6 9.3 collective-permute-start.1
  502.9 48.1 %reduce-scatter.2.cloned.1.call-start = ((), (), s32[]{:S(2)}) async-start(), calls=%async_computation.1 | async-start | bytes 655360 | tf_op jit(solution)/shard_map/while/body/eval_jaxpr/reduce_scatter | solution.py:182
  557.5 48.1 %reduce-scatter.2.cloned.1.call-start = ((), (), s32[]{:S(2)}) async-start(), calls=%async_computation.1 | async-start | bytes 655360 | tf_op jit(solution)/shard_map/while/body/eval_jaxpr/reduce_scatter | solution.py:182
  612.1 47.4 %reduce-scatter.2.cloned.1.call-start = ((), (), s32[]{:S(2)}) async-start(), calls=%async_computation.1 | async-start | bytes 655360 | tf_op jit(solution)/shard_map/while/body/eval_jaxpr/reduce_scatter | solution.py:182
  666.0 48.2 %reduce-scatter.2.cloned.1.call-start = ((), (), s32[]{:S(2)}) async-start(), calls=%async_computation.1 | async-start | bytes 655360 | tf_op jit(solution)/shard_map/while/body/eval_jaxpr/reduce_scatter | solution.py:182
  720.7 47.3 %reduce-scatter.2.cloned.1.call-start = ((), (), s32[]{:S(2)}) async-start(), calls=%async_computation.1 | async-start | bytes 655360 | tf_op jit(solution)/shard_map/while/body/eval_jaxpr/reduce_scatter | solution.py:182
  774.4 48.1 %reduce-scatter.2.cloned.1.call-start = ((), (), s32[]{:S(2)}) async-start(), calls=%async_computation.1 | async-start | bytes 655360 | tf_op jit(solution)/shard_map/while/body/eval_jaxpr/reduce_scatter | solution.py:182
  829.0 47.4 %reduce-scatter.2.cloned.1.call-start = ((), (), s32[]{:S(2)}) async-start(), calls=%async_computation.1 | async-start | bytes 655360 | tf_op jit(solution)/shard_map/while/body/eval_jaxpr/reduce_scatter | solution.py:182
  883.0 48.1 %reduce-scatter.2.cloned.1.call-start = ((), (), s32[]{:S(2)}) async-start(), calls=%async_computation.1 | async-start | bytes 655360 | tf_op jit(solution)/shard_map/while/body/eval_jaxpr/reduce_scatter | solution.py:182
  937.6 47.3 %reduce-scatter.2.cloned.1.call-start = ((), (), s32[]{:S(2)}) async-start(), calls=%async_computation.1 | async-start | bytes 655360 | tf_op jit(solution)/shard_map/while/body/eval_jaxpr/reduce_scatter | solution.py:182
  991.4 48.1 %reduce-scatter.2.cloned.1.call-start = ((), (), s32[]{:S(2)}) async-start(), calls=%async_computation.1 | async-start | bytes 655360 | tf_op jit(solution)/shard_map/while/body/eval_jaxpr/reduce_scatter | solution.py:182
  1039.5 6.5 collective-permute-start.1
  (16 other events, 87.4 us)
Sparse Core Ops, SparseCore 0:
  469.5 23.8 reduce-scatter.1
  522.9 23.7 reduce-scatter.1
  577.5 22.9 reduce-scatter.1
  632.1 22.2 reduce-scatter.1
  686.0 23.0 reduce-scatter.1
  740.7 21.9 reduce-scatter.1
  794.5 22.9 reduce-scatter.1
  849.1 22.2 reduce-scatter.1
  903.0 22.9 reduce-scatter.1
  957.7 21.8 reduce-scatter.1
  1011.4 22.9 reduce-scatter.1
where the time goes:
time: 1070 us; the launch traced here: 1060 us
  blocking collectives  360 us (34%)
  local copies, waits for them, and re-layouts  233 us (22%)
  other arithmetic  189 us (18%)
  matrix products  132 us (12%)
  starting transfers between devices  93.6 us (9%)
  waiting for transfers between devices  36.5 us (3%)
  between operations  13.8 us (1%)
    all_gather x11, blocking collectives, backward_tick(): lax.all_gather(for_sending(own_input), 'filt', axis=0, tiled=True)  215 us
    all_gather x11, blocking collectives, forward_tick(): lax.all_gather(a, 'filt', axis=0, tiled=True)  144 us
    while x253, other arithmetic  107 us
    dot_general x11, local copies, waits for them, and re-layouts, forward_tick(): jnp.einsum('ki,irz->krz', columns, panel_part, preferred_element_type=jnp...  104 us
    ppermute x22, starting transfers between devices, passed_along(): lax.ppermute(value, axis, [(source, source + steps) for source in range(f...  93.5 us
    dot_general x11, matrix products, backward_tick(): jnp.einsum('krz,irz->ki', stacked, lax.all_gather(for_sending(own_input),...  40.4 us
    dynamic_slice x33, local copies, waits for them, and re-layouts, store_slot(): previous = lax.dynamic_index_in_dim(buffer, position, 0, keepdims=False)  38 us
    ppermute x22, waiting for transfers between devices, passed_along(): lax.ppermute(value, axis, [(source, source + steps) for source in range(f...  36.3 us
  transfers between devices with their start and end apart: 33, of which 22 were waited for; matrix products, arithmetic and copies ran while one was open for 12% of the time, Pallas kernels for 0%

commit v1 on v0

--- a/solution.py
+++ b/solution.py
@@ -8,6 +8,28 @@
 tap_offsets = [
     (first, second, third) for first in (-1, 0, 1) for second in (-1, 0, 1) for third in (-1, 0, 1)
 ]
+
+
+def in_order(tiles, dim):
+    tiles = jnp.moveaxis(tiles, 0, dim)
+    shape = tiles.shape
+    return tiles.reshape(*shape[:dim], shape[dim] * shape[dim + 1], *shape[dim + 2 :])
+
+
+def gather_around(x, axis, dim):
+    size = lax.axis_size(axis)
+    pairs = [(i, (i + 1) % size) for i in range(size)]
+    back = [(b, a) for a, b in pairs]
+    lower, upper = ([], [])
+    for step in range(size - 1):
+        if step % 2 == 0:
+            lower.append(lax.ppermute(lower[-1] if lower else x, axis, pairs))
+        else:
+            upper.append(lax.ppermute(upper[-1] if upper else x, axis, back))
+    blocks = jnp.stack([*lower[::-1], x, *upper])
+    shift = lax.axis_index(axis) - len(lower)
+    blocks = blocks[(jnp.arange(size) - shift) % size]
+    return in_order(blocks, dim)
 
 
 def passed_along(value, axis, steps):
@@ -132,9 +154,7 @@
         position = jnp.clip(sample, 0, micro_count - 1)
         first_input = lax.dynamic_index_in_dim(flat_volumes, position, 0, keepdims=False)
         own_input = jnp.where(section_pos == 0, first_input, incoming)
-        panel_part = jax.tree.map(
-            lambda a: lax.all_gather(a, "filt", axis=0, tiled=True), own_input
-        )
+        panel_part = jax.tree.map(lambda a: gather_around(a, "filt", 0), own_input)
         columns = lax.slice_in_dim(weight_rows, 0, panel_part.shape[0], axis=1)
         product = jnp.zeros(
             (own_count * tap_count, row_total, lane_count), jnp.float32

time: 1070 us -> 1060 us (level)
  blocking collectives: 360 us -> 203 us
  waiting for transfers between devices: 36.5 us -> 134 us
  starting transfers between devices: 93.6 us -> 130 us
  other arithmetic: 189 us -> 201 us
    all_gather x11 -> x0, blocking collectives: 144 us -> none  [forward_tick(): lax.all_gather(a, 'filt', axis=0, tiled=True)]
    ppermute x0 -> x33, waiting for transfers between devices: none -> 77.9 us  [the longest x22 76.4 us: gather_around(): lower.append(lax.ppermute(lower[-1] if lower else x, axis, pairs))]
    ppermute x0 -> x33, starting transfers between devices: none -> 36.8 us  [the longest x11 34.6 us: gather_around(): upper.append(lax.ppermute(upper[-1] if upper else x, axis, back))]
    ppermute x22, waiting for transfers between devices: 36.3 us -> 56 us  [passed_along(): lax.ppermute(value, axis, [(source, source + steps) for source in range(f...]
    dynamic_slice x11 -> x22, local copies, waits for them, and re-layouts: 17.1 us -> 34.5 us  [backward_tick(): own_input = lax.dynamic_index_in_dim(stored, position, 0, keepdims=False)]
    all_gather x11, blocking collectives: 215 us -> 203 us  [backward_tick(): lax.all_gather(for_sending(own_input), 'filt', axis=0, tiled=True)]
  transfers between devices with their start and end apart: 33 -> 66, of which waited for: 22 -> 45; matrix products, arithmetic and copies ran while one was open for 12% -> 14% of each run, Pallas kernels for 0% -> 0%
where the time goes in v1:
time: 1060 us; the launch traced here: 1050 us
  local copies, waits for them, and re-layouts  232 us (22%)
  blocking collectives  203 us (19%)
  other arithmetic  201 us (19%)
  matrix products  136 us (13%)
  waiting for transfers between devices  134 us (13%)
  starting transfers between devices  130 us (12%)
  between operations  13.8 us (1%)
    all_gather x11, blocking collectives, backward_tick(): lax.all_gather(for_sending(own_input), 'filt', axis=0, tiled=True)  203 us
    while x253, other arithmetic  107 us
    dot_general x11, local copies, waits for them, and re-layouts, forward_tick(): jnp.einsum('ki,irz->krz', columns, panel_part, preferred_element_type=jnp...  104 us
    ppermute x22, starting transfers between devices, passed_along(): lax.ppermute(value, axis, [(source, source + steps) for source in range(f...  93.4 us
    ppermute x22, waiting for transfers between devices, gather_around(): lower.append(lax.ppermute(lower[-1] if lower else x, axis, pairs))  76.4 us
    ppermute x22, waiting for transfers between devices, passed_along(): lax.ppermute(value, axis, [(source, source + steps) for source in range(f...  56 us
    dynamic_update_slice x33, other arithmetic, store_slot(): lax.dynamic_update_index_in_dim(buffer, jnp.where(in_range, entry, previo...  44.3 us
    dot_general x11, matrix products, backward_tick(): jnp.einsum('krz,irz->ki', stacked, lax.all_gather(for_sending(own_input),...  40.4 us
  transfers between devices with their start and end apart: 66, of which 45 were waited for; matrix products, arithmetic and copies ran while one was open for 14% of the time, Pallas kernels for 0%

profile of v1, /device:TPU:1, one launch (start us, length us, event | category | flops | bytes accessed | tf_op | source)
XLA Modules:
  0.0 1051.1 jit_solution(13681950284693477151)
XLA Ops:
  12.8 423.1 %while.45 = (s32[]{:T(128)}, bf16[64,8,128]{2,1,0:T(8,128)(2,1)S(1)}, f32[8,64,8,128]{3,2,1,0:T(8,128)}, bf16[8,64,8,128]{3,2,1,0:T(8,128)(2,1)}, pred[]{:T(512)...) while((s32[]{:T(128)}, ...), condition=%wide.region_1.2_spmd.clone.clone, body=%wide.region_0.1_spmd.sunk.clone.clone.sunk | while | flops 1111983360 | bytes 49661480 | solution.py:174
  31.3 9.4 copy.216
  70.0 9.4 copy.216
  107.8 9.4 copy.216
  146.1 9.4 copy.216
  184.4 9.4 copy.216
  222.7 9.4 copy.216
  261.1 9.4 copy.216
  299.4 9.4 copy.216
  337.7 9.4 copy.216
  376.1 9.4 copy.216
  414.4 9.4 copy.216
  437.1 600.4 %while.46 = (s32[]{:T(128)}, bf16[64,8,128]{2,1,0:T(8,128)(2,1)S(1)}, f32[1728,256]{1,0:T(8,128)}, f32[64]{0:T(128)}, bf16[8,64,8,128]{3,2,1,0:T(8,128)(2,1)}, /...) while((s32[]{:T(128)}, ...), condition=%wide.region_5.6_spmd.clone.clone.clone, body=%wide.region_2.5_spmd.sunk.clone.clone.clone.sunk | while | flops 1849737728 | bytes 33268696 | solution.py:221
  460.9 17.6 %all-gather.4 = bf16[1,256,8,128]{3,1,2,0:T(8,128)(2,1)S(1)} all-gather(bf16[1,64,8,128]{3,1,2,0:T(8,128)(2,1)} %copy.221), channel_id=2, replica_groups=mesh['groups'=2,'section'=4,'filt'=4] {'filt'}, dimensions={1}, use_global_device_ids=true | all-gather | bytes 655360 | tf_op jit(solution)/shard_map/while/body/eval_jaxpr/all_gather | solution.py:194
  513.6 19.9 %all-gather.4 = bf16[1,256,8,128]{3,1,2,0:T(8,128)(2,1)S(1)} all-gather(bf16[1,64,8,128]{3,1,2,0:T(8,128)(2,1)} %copy.221), channel_id=2, replica_groups=mesh['groups'=2,'section'=4,'filt'=4] {'filt'}, dimensions={1}, use_global_device_ids=true | all-gather | bytes 655360 | tf_op jit(solution)/shard_map/while/body/eval_jaxpr/all_gather | solution.py:194
  568.9 19.2 %all-gather.4 = bf16[1,256,8,128]{3,1,2,0:T(8,128)(2,1)S(1)} all-gather(bf16[1,64,8,128]{3,1,2,0:T(8,128)(2,1)} %copy.221), channel_id=2, replica_groups=mesh['groups'=2,'section'=4,'filt'=4] {'filt'}, dimensions={1}, use_global_device_ids=true | all-gather | bytes 655360 | tf_op jit(solution)/shard_map/while/body/eval_jaxpr/all_gather | solution.py:194
  623.5 19.0 %all-gather.4 = bf16[1,256,8,128]{3,1,2,0:T(8,128)(2,1)S(1)} all-gather(bf16[1,64,8,128]{3,1,2,0:T(8,128)(2,1)} %copy.221), channel_id=2, replica_groups=mesh['groups'=2,'section'=4,'filt'=4] {'filt'}, dimensions={1}, use_global_device_ids=true | all-gather | bytes 655360 | tf_op jit(solution)/shard_map/while/body/eval_jaxpr/all_gather | solution.py:194
  678.4 18.6 %all-gather.4 = bf16[1,256,8,128]{3,1,2,0:T(8,128)(2,1)S(1)} all-gather(bf16[1,64,8,128]{3,1,2,0:T(8,128)(2,1)} %copy.221), channel_id=2, replica_groups=mesh['groups'=2,'section'=4,'filt'=4] {'filt'}, dimensions={1}, use_global_device_ids=true | all-gather | bytes 655360 | tf_op jit(solution)/shard_map/while/body/eval_jaxpr/all_gather | solution.py:194
  733.0 18.5 %all-gather.4 = bf16[1,256,8,128]{3,1,2,0:T(8,128)(2,1)S(1)} all-gather(bf16[1,64,8,128]{3,1,2,0:T(8,128)(2,1)} %copy.221), channel_id=2, replica_groups=mesh['groups'=2,'section'=4,'filt'=4] {'filt'}, dimensions={1}, use_global_device_ids=true | all-gather | bytes 655360 | tf_op jit(solution)/shard_map/while/body/eval_jaxpr/all_gather | solution.py:194
  787.8 18.1 %all-gather.4 = bf16[1,256,8,128]{3,1,2,0:T(8,128)(2,1)S(1)} all-gather(bf16[1,64,8,128]{3,1,2,0:T(8,128)(2,1)} %copy.221), channel_id=2, replica_groups=mesh['groups'=2,'section'=4,'filt'=4] {'filt'}, dimensions={1}, use_global_device_ids=true | all-gather | bytes 655360 | tf_op jit(solution)/shard_map/while/body/eval_jaxpr/all_gather | solution.py:194
  842.4 18.1 %all-gather.4 = bf16[1,256,8,128]{3,1,2,0:T(8,128)(2,1)S(1)} all-gather(bf16[1,64,8,128]{3,1,2,0:T(8,128)(2,1)} %copy.221), channel_id=2, replica_groups=mesh['groups'=2,'section'=4,'filt'=4] {'filt'}, dimensions={1}, use_global_device_ids=true | all-gather | bytes 655360 | tf_op jit(solution)/shard_map/while/body/eval_jaxpr/all_gather | solution.py:194
  897.3 17.8 %all-gather.4 = bf16[1,256,8,128]{3,1,2,0:T(8,128)(2,1)S(1)} all-gather(bf16[1,64,8,128]{3,1,2,0:T(8,128)(2,1)} %copy.221), channel_id=2, replica_groups=mesh['groups'=2,'section'=4,'filt'=4] {'filt'}, dimensions={1}, use_global_device_ids=true | all-gather | bytes 655360 | tf_op jit(solution)/shard_map/while/body/eval_jaxpr/all_gather | solution.py:194
  951.8 18.1 %all-gather.4 = bf16[1,256,8,128]{3,1,2,0:T(8,128)(2,1)S(1)} all-gather(bf16[1,64,8,128]{3,1,2,0:T(8,128)(2,1)} %copy.221), channel_id=2, replica_groups=mesh['groups'=2,'section'=4,'filt'=4] {'filt'}, dimensions={1}, use_global_device_ids=true | all-gather | bytes 655360 | tf_op jit(solution)/shard_map/while/body/eval_jaxpr/all_gather | solution.py:194
  1006.6 17.8 %all-gather.4 = bf16[1,256,8,128]{3,1,2,0:T(8,128)(2,1)S(1)} all-gather(bf16[1,64,8,128]{3,1,2,0:T(8,128)(2,1)} %copy.221), channel_id=2, replica_groups=mesh['groups'=2,'section'=4,'filt'=4] {'filt'}, dimensions={1}, use_global_device_ids=true | all-gather | bytes 655360 | tf_op jit(solution)/shard_map/while/body/eval_jaxpr/all_gather | solution.py:194
  (784 shorter events, 728.7 us)
Async XLA Ops:
  44.3 8.4 collective-permute-start.3
  83.0 8.1 collective-permute-start.3
  120.8 8.6 collective-permute-start.3
  159.1 8.6 collective-permute-start.3
  197.4 8.6 collective-permute-start.3
  235.7 8.6 collective-permute-start.3
  274.1 8.6 collective-permute-start.3
  312.4 8.6 collective-permute-start.3
  350.7 8.6 collective-permute-start.3
  389.0 8.6 collective-permute-start.3
  427.4 8.6 collective-permute-start.3
  437.1 44.4 %reduce-scatter.2.cloned.1.call-start = ((), (), s32[]{:S(2)}) async-start(), calls=%async_computation.1 | async-start | bytes 655360 | tf_op jit(solution)/shard_map/while/body/eval_jaxpr/reduce_scatter | solution.py:202
  481.5 8.4 collective-permute-start.4
  489.9 48.7 %reduce-scatter.2.cloned.1.call-start = ((), (), s32[]{:S(2)}) async-start(), calls=%async_computation.1 | async-start | bytes 655360 | tf_op jit(solution)/shard_map/while/body/eval_jaxpr/reduce_scatter | solution.py:202
  545.1 48.0 %reduce-scatter.2.cloned.1.call-start = ((), (), s32[]{:S(2)}) async-start(), calls=%async_computation.1 | async-start | bytes 655360 | tf_op jit(solution)/shard_map/while/body/eval_jaxpr/reduce_scatter | solution.py:202
  599.8 47.8 %reduce-scatter.2.cloned.1.call-start = ((), (), s32[]{:S(2)}) async-start(), calls=%async_computation.1 | async-start | bytes 655360 | tf_op jit(solution)/shard_map/while/body/eval_jaxpr/reduce_scatter | solution.py:202
  654.7 47.5 %reduce-scatter.2.cloned.1.call-start = ((), (), s32[]{:S(2)}) async-start(), calls=%async_computation.1 | async-start | bytes 655360 | tf_op jit(solution)/shard_map/while/body/eval_jaxpr/reduce_scatter | solution.py:202
  709.2 47.4 %reduce-scatter.2.cloned.1.call-start = ((), (), s32[]{:S(2)}) async-start(), calls=%async_computation.1 | async-start | bytes 655360 | tf_op jit(solution)/shard_map/while/body/eval_jaxpr/reduce_scatter | solution.py:202
  764.1 47.0 %reduce-scatter.2.cloned.1.call-start = ((), (), s32[]{:S(2)}) async-start(), calls=%async_computation.1 | async-start | bytes 655360 | tf_op jit(solution)/shard_map/while/body/eval_jaxpr/reduce_scatter | solution.py:202
  818.6 46.9 %reduce-scatter.2.cloned.1.call-start = ((), (), s32[]{:S(2)}) async-start(), calls=%async_computation.1 | async-start | bytes 655360 | tf_op jit(solution)/shard_map/while/body/eval_jaxpr/reduce_scatter | solution.py:202
  873.5 46.6 %reduce-scatter.2.cloned.1.call-start = ((), (), s32[]{:S(2)}) async-start(), calls=%async_computation.1 | async-start | bytes 655360 | tf_op jit(solution)/shard_map/while/body/eval_jaxpr/reduce_scatter | solution.py:202
  928.1 46.9 %reduce-scatter.2.cloned.1.call-start = ((), (), s32[]{:S(2)}) async-start(), calls=%async_computation.1 | async-start | bytes 655360 | tf_op jit(solution)/shard_map/while/body/eval_jaxpr/reduce_scatter | solution.py:202
  982.8 46.7 %reduce-scatter.2.cloned.1.call-start = ((), (), s32[]{:S(2)}) async-start(), calls=%async_computation.1 | async-start | bytes 655360 | tf_op jit(solution)/shard_map/while/body/eval_jaxpr/reduce_scatter | solution.py:202
  1029.5 7.9 collective-permute-start.4
  (48 other events, 297.8 us)
Sparse Core Ops, SparseCore 0:
  456.3 22.3 reduce-scatter.1
  509.1 24.3 reduce-scatter.1
  564.3 23.7 reduce-scatter.1
  619.0 23.5 reduce-scatter.1
  673.8 22.9 reduce-scatter.1
  728.4 22.7 reduce-scatter.1
  783.2 21.7 reduce-scatter.1
  837.8 21.2 reduce-scatter.1
  892.6 20.7 reduce-scatter.1
  947.2 21.2 reduce-scatter.1
  1002.0 20.8 reduce-scatter.1
